TPU v7x, 32 devices: a whole 2x2x4 slice. The times are simulated.
32 devices in a mesh: groups: 2 (over y), video: 4 (over z), tensor: 4 (over x, core).
Axes of the slice: x: 2, y: 2, z: 4, core: 2. Of those that a mesh axis runs over, the one named last changes fastest.
Arguments:
- frames: bfloat16 [24, 256, 6144], P(('groups', 'video')), parts along dimension 0, may hold values from -610 to 610
- frame_video: int32 [24], P(('groups', 'video')), parts along dimension 0, may hold values from 0 to 3, never falling along the last dimension, each value on 1 to 6 neighbouring positions
- qkv_weight: bfloat16 [6144, 3, 3072], P('video', None, 'tensor'), may hold values from -0.078125 to 0.078125
- conn_weight: bfloat16 [3072, 3, 4096], P('tensor', None, 'video'), may hold values from -6 to 6
Outputs:
- summary: bfloat16 [384, 4096], P(('groups', 'video'), 'tensor'), parts along dimension 0
There are 2 independent parts, one for each index of `groups`. A program takes and returns all parts, laid end to end along the dimension named above; an argument that names none is the same for every part. Nothing has to cross between parts.
All inputs are finite; a program needn't handle non-finite values.
Results may differ from a plain program's by a relative error of at most 0.009.
Values may be sent and summed in bfloat16 or wider, within the bound.
No kernel may reach another device: no remote copies, remote signals or barrier semaphores. Data moves between devices by JAX's collectives and lax.ppermute only.
A program may use at most 192 MiB of HBM per device.

v0:
```python
import math
import jax
import jax.numpy as jnp
from jax import lax
from jax.sharding import PartitionSpec as P

HD = 128
PATCH = 256
POOL = 16


def rms_norm(values):
    return values * lax.rsqrt(jnp.mean(values * values, axis=-1, keepdims=True) + 1e-06)


def head_chunks(heads):
    if heads >= 4 and heads % 2 == 0:
        return [1] + [2] * ((heads - 2) // 2) + [1]
    return [1] * heads


def moved_weights(chunk, n_video, after=None):
    v = lax.axis_index("video")
    g = lax.axis_index("groups")
    half = chunk.shape[0] // 2
    mine = lax.dynamic_slice_in_dim(chunk, g * half, half, axis=0)
    if after is not None:
        mine, after = lax.optimization_barrier((mine, after))
    other = lax.dynamic_slice_in_dim(chunk, (1 - g) * half, half, axis=0)
    gathered = lax.all_gather(mine, "video", axis=0, tiled=True)
    onward = jnp.concatenate(
        [
            lax.dynamic_slice_in_dim(gathered, (v + 1 + i) % n_video * half, half, axis=0)
            for i in range(n_video - 1)
        ],
        axis=0,
    )
    return ([other, gathered, onward], after)


def forward(onward):
    return lax.ppermute(onward, "groups", [(0, 1), (1, 0)])


def attend(proj, nframes, heads, scale, blocks, inner):
    proj = proj.reshape(nframes, PATCH, 3, heads, HD)
    query = rms_norm(proj[:, :, 0]).astype(jnp.bfloat16)
    keys = rms_norm(proj[:, :, 1]).astype(jnp.bfloat16)
    values = proj[:, :, 2].astype(jnp.bfloat16)
    scores = jnp.einsum("fphd,fkhd->fhpk", query, keys, preferred_element_type=jnp.float32) * scale
    probs = jnp.exp(scores)
    probs = (probs / jnp.sum(probs, axis=-1, keepdims=True)).astype(jnp.bfloat16)
    attended = jnp.einsum("fhpk,fkhd->fphd", probs, values, preferred_element_type=jnp.float32)
    grid = attended.reshape(nframes, blocks, inner, blocks, inner, heads, HD)
    return jnp.mean(grid, axis=(2, 4)).reshape(nframes * POOL, heads * HD).astype(jnp.bfloat16)


def per_device(frames, frame_video, qkv_weight, conn_weight):
    scale = 1.0 / math.sqrt(HD)
    blocks = math.isqrt(POOL)
    inner = math.isqrt(PATCH) // blocks
    nframes = frames.shape[0]
    patch_rows = nframes * PATCH
    n_video = lax.axis_size("video")
    assert lax.axis_size("groups") == 2
    v = lax.axis_index("video")
    g = lax.axis_index("groups")
    heads_local = qkv_weight.shape[2] // HD
    sizes = head_chunks(heads_local)
    moved = []
    first = 0
    for size in sizes:
        chunk = qkv_weight[:, :, first * HD : (first + size) * HD]
        first += size
        if len(moved) == len(sizes) - 1 and len(sizes) > 2:
            whole_rows, moved[-1][1] = lax.optimization_barrier((chunk, moved[-1][1]))
            step = [lax.all_gather(whole_rows, "video", axis=0, tiled=True), None, None]
        elif moved:
            step, moved[-1][1] = moved_weights(chunk, n_video, after=moved[-1][1])
            step.append(forward(step[2]))
        else:
            step, _ = moved_weights(chunk, n_video)
            step.append(forward(step[2]))
            step[3], frames = lax.optimization_barrier((step[3], frames))
        moved.append(step)
    wide = frames.astype(jnp.float32)
    center = wide - jnp.mean(wide, axis=-1, keepdims=True)
    normed = center * lax.rsqrt(jnp.mean(center * center, axis=-1, keepdims=True) + 1e-06)
    normed = normed.astype(jnp.bfloat16).reshape(patch_rows, frames.shape[2])
    local_rows = qkv_weight.shape[0]
    half = local_rows // 2

    def columns(shard, which):
        return lax.dynamic_slice_in_dim(normed, shard * local_rows + which * half, half, axis=1)

    own_half = jnp.concatenate([columns(u, g) for u in range(n_video)], axis=1)
    own_piece = columns(v, 1 - g)
    rolled = jnp.concatenate(
        [columns((v + 1 + i) % n_video, 1 - g) for i in range(n_video - 1)], axis=1
    )
    if len(moved) > 2 and moved[1][3] is not None:
        moved[1][3], own_half = lax.optimization_barrier((moved[1][3], own_half))
    ids = [frame_video] + [
        lax.ppermute(frame_video, "video", [(a, (a + k) % n_video) for a in range(n_video)])
        for k in range(1, n_video)
    ]
    ids_from = jnp.argsort(jnp.stack([(v - k) % n_video for k in range(n_video)]))
    video_all = jnp.take(jnp.stack(ids), ids_from, axis=0).reshape(-1)
    pooled_parts = []
    for index, size in enumerate(sizes):
        width = 3 * size * HD
        if moved[index][1] is None:
            full = moved[index][0].reshape(n_video * 2 * half, width)
            proj = jnp.dot(normed, full, preferred_element_type=jnp.float32)
            pooled_parts.append(attend(proj, nframes, size, scale, blocks, inner))
            continue
        other, gathered, onward, received = moved[index]
        if index == 0:
            video_all, received = lax.optimization_barrier((video_all, received))
        proj = jnp.dot(own_piece, other.reshape(half, width), preferred_element_type=jnp.float32)
        proj = proj + jnp.dot(
            own_half, gathered.reshape(n_video * half, width), preferred_element_type=jnp.float32
        )
        proj = proj + jnp.dot(
            rolled,
            received.reshape((n_video - 1) * half, width),
            preferred_element_type=jnp.float32,
        )
        pooled_parts.append(attend(proj, nframes, size, scale, blocks, inner))
    pooled = jnp.concatenate(pooled_parts, axis=1)
    shifted = [pooled] + [
        lax.ppermute(pooled, "video", [(a, (a + k) % n_video) for a in range(n_video)])
        for k in range(1, n_video)
    ]
    came_from = jnp.argsort(jnp.stack([(v - k) % n_video for k in range(n_video)]))
    pooled_all = jnp.take(jnp.stack(shifted), came_from, axis=0).reshape(-1, pooled.shape[1])
    rows = pooled_all.shape[0]
    partial_proj = jnp.einsum(
        "rc,ckt->rkt", pooled_all, conn_weight, preferred_element_type=jnp.float32
    )
    n_tensor = lax.axis_size("tensor")
    t = lax.axis_index("tensor")
    sent = partial_proj.astype(jnp.bfloat16)
    block = rows // n_tensor
    total = lax.dynamic_slice_in_dim(sent, t * block, block, axis=0).astype(jnp.float32)
    for k in range(1, n_tensor):
        piece = lax.dynamic_slice_in_dim(sent, (t + k) % n_tensor * block, block, axis=0)
        got = lax.ppermute(piece, "tensor", [(a, (a + k) % n_tensor) for a in range(n_tensor)])
        total = total + got.astype(jnp.float32)
    clip_rows = total.astype(jnp.bfloat16)
    if n_video == n_tensor:
        pieces = [None] * n_tensor
        for k in range(n_tensor):
            pairs = [
                (a * n_tensor + b, (b + k) % n_tensor * n_tensor + a)
                for a in range(n_video)
                for b in range(n_tensor)
            ]
            got = lax.ppermute(clip_rows, ("video", "tensor"), pairs)
            pieces[k] = got
        source = [(v - k) % n_tensor for k in range(n_tensor)]
        stacked = jnp.stack(pieces, axis=0)
        order = jnp.argsort(jnp.stack(source))
        clip_proj = jnp.take(stacked, order, axis=0).reshape(rows, 3, -1).astype(jnp.float32)
    else:
        clip_rows = lax.all_gather(clip_rows, "video", axis=0, tiled=False)
        sub = n_video // n_tensor
        clip_rows = clip_rows.reshape((n_tensor, sub) + clip_rows.shape[1:])
        clip_proj = lax.all_to_all(clip_rows, "tensor", 0, 0, tiled=False)
        clip_proj = jnp.transpose(clip_proj, (0, 2, 3, 1, 4))
        clip_proj = clip_proj.reshape(rows, 3, -1).astype(jnp.float32)
    t_heads = clip_proj.shape[2] // HD
    out_rows = rows // n_video
    start = v * out_rows
    own = lax.dynamic_slice_in_dim(clip_proj[:, 0], start, out_rows, axis=0)
    tquery = rms_norm(own.reshape(out_rows, t_heads, HD)).astype(jnp.bfloat16)
    tkey = rms_norm(clip_proj[:, 1].reshape(rows, t_heads, HD)).astype(jnp.bfloat16)
    tvalue = clip_proj[:, 2].reshape(rows, t_heads, HD).astype(jnp.bfloat16)
    seg_rows = jnp.repeat(video_all, POOL)
    row_frame = jnp.arange(rows, dtype=jnp.int32) // POOL
    own_seg = lax.dynamic_slice_in_dim(seg_rows, start, out_rows)
    own_frame = lax.dynamic_slice_in_dim(row_frame, start, out_rows)
    allowed = (seg_rows[None, :] == own_seg[:, None]) & (row_frame[None, :] <= own_frame[:, None])
    logits = jnp.einsum("rhd,khd->hrk", tquery, tkey, preferred_element_type=jnp.float32) * scale
    weights = jnp.where(allowed[None], jnp.exp(logits), jnp.float32(0.0))
    numer = jnp.einsum(
        "hrk,khd->rhd", weights.astype(jnp.bfloat16), tvalue, preferred_element_type=jnp.float32
    )
    denom = jnp.sum(weights, axis=-1)
    summary = numer / jnp.transpose(denom)[:, :, None]
    return summary.reshape(out_rows, t_heads * HD).astype(jnp.bfloat16)


def solution(mesh):
    return jax.shard_map(
        per_device,
        mesh=mesh,
        in_specs=(
            P(("groups", "video"), None, None),
            P(("groups", "video")),
            P("video", None, "tensor"),
            P("tensor", None, "video"),
        ),
        out_specs=P(("groups", "video"), "tensor"),
        check_vma=False,
    )
```

profile of v0, /device:TPU:10, one launch (start us, length us, event | category | flops | bytes accessed | tf_op | source)
XLA Modules:
  0.0 423.8 jit_solution(11651524342442306222)
XLA Ops:
  6.5 2.8 fusion.67
  11.4 2.7 fusion.68
  18.0 43.6 %all-gather.5.cloned.1.call-done = bf16[3072,3,128]{0,2,1:T(8,128)(2,1)} async-done(((bf16[768,3,128]{0,2,1:T(8,128)(2,1)}), bf16[3072,3,128]{0,2,1:T(8,128)(2,1)}) %all-gather.5.cloned.1.call-update) | async-done | bytes 2359312 | tf_op jit(solution)/shard_map/all_gather | solution.py:30
  68.2 3.5 collective-permute-start.3
  82.2 22.9 %collective-permute-done = bf16[2304,3,128]{0,2,1:T(8,128)(2,1)} collective-permute-done((bf16[2304,3,128]{0,2,1:T(8,128)(2,1)}, bf16[2304,3,128]{0,2,1:T(8,128)(2,1)}, u32[]{:S(2)}, u32[]{:S(2)}) %collective-permute-start) | collective-permute-done | bytes 1769504 | tf_op jit(solution)/shard_map/ppermute | solution.py:42
  105.0 5.1 %convert_reduce_fusion = f32[3,256]{1,0:T(4,128)S(1)} fusion(bf16[3,256,6144]{2,1,0:T(8,128)(2,1)} %param.4), kind=kLoop, calls=%fused_computation.4 | loop fusion | flops 9436416 | bytes 9440256 | tf_op jit(solution)/shard_map/reduce_sum | solution.py:87
  110.2 6.3 %fusion.2 = f32[3,256]{1,0:T(4,128)S(1)} fusion(bf16[3,256,6144]{2,1,0:T(8,128)(2,1)} %param.4, f32[3,256]{1,0:T(4,128)S(1)} %broadcast_multiply_fusion), kind=kLoop, calls=%fused_computation.7 | loop fusion | flops 18873600 | bytes 9443328 | tf_op jit(solution)/shard_map/reduce_sum | solution.py:88
  116.5 34.0 %all-gather.7.cloned.1.call-done = bf16[3072,3,256]{0,2,1:T(8,128)(2,1)} async-done(((bf16[768,3,256]{0,2,1:T(8,128)(2,1)}), bf16[3072,3,256]{0,2,1:T(8,128)(2,1)}) %all-gather.7.cloned.1.call-update) | async-done | bytes 4718608 | tf_op jit(solution)/shard_map/all_gather | solution.py:30
  155.1 12.2 %fusion.3 = bf16[3,256,6144]{2,1,0:T(8,128)(2,1)} fusion(bf16[3,256,6144]{2,1,0:T(8,128)(2,1)} %param.4, f32[3,256]{1,0:T(4,128)S(1)} %add_rsqrt_fusion.10, f32[3,256]{1,0:T(4,128)S(1)} %broadcast_multiply_fusion), kind=kLoop, calls=%fused_computation.8 | loop fusion | flops 18874368 | bytes 18880512 | tf_op jit(solution)/shard_map/convert_element_type | solution.py:89
  169.7 4.0 fusion.22
  173.7 3.8 fusion.20
  177.5 2.5 constant_dynamic-slice_fusion.11
  183.3 3.7 fusion.65
  186.9 45.1 %collective-permute-done.1 = bf16[2304,3,256]{0,2,1:T(8,128)(2,1)} collective-permute-done((bf16[2304,3,256]{0,2,1:T(8,128)(2,1)S(1)}, bf16[2304,3,256]{0,2,1:T(8,128)(2,1)}, u32[]{:S(2)}, u32[]{:S(2)}) %collective-permute-start.1) | collective-permute-done | bytes 3538976 | tf_op jit(solution)/shard_map/ppermute | solution.py:42
  232.0 2.7 fusion.12
  236.2 3.3 multiply_reduce_fusion.8
  240.4 7.1 %fusion.72 = f32[768,768]{1,0:T(8,128)S(1)} fusion(bf16[768,3072]{1,0:T(8,128)(2,1)} %copy-done.1, bf16[3072,768]{0,1:T(8,128)(2,1)} %bitcast.191), kind=kOutput, calls=%fused_computation.180 | convolution fusion | flops 3623878656 | bytes 11796480 | tf_op jit(solution)/shard_map/dot_general | solution.py:121
  253.9 6.6 %add_add_fusion.1 = f32[768,768]{1,0:T(8,128)} fusion(f32[768,768]{1,0:T(8,128)S(1)} %copy-done.19, f32[768,768]{1,0:T(8,128)S(1)} %fusion.72, bf16[2304,768]{0,1:T(8,128)(2,1)} %bitcast.21, bf16[768,768]{1,0:T(8,128)(2,1)S(1)} %copy-done.10, bf16[768,768]{1,0:T(8,128)(2,1)S(1)} %copy-done.13, bf16[768,768]{1,0:T(8,128)(2,1)S(1)} %copy-done.7), kind=kOutput, calls=%fused_computation.17 | convolution fusion | flops 2729705472 | bytes 14155776 | tf_op jit(solution)/shard_map/dot_general | solution.py:124
  260.5 2.9 reshape.426
  267.5 7.5 %fusion.73 = f32[768,768]{1,0:T(8,128)S(1)} fusion(bf16[768,3072]{1,0:T(8,128)(2,1)} %copy-done.1, bf16[3072,768]{0,1:T(8,128)(2,1)} %bitcast.192), kind=kOutput, calls=%fused_computation.181 | convolution fusion | flops 3623878656 | bytes 11796480 | tf_op jit(solution)/shard_map/dot_general | solution.py:121
  275.0 54.6 %collective-permute-done.5 = bf16[2304,3,256]{0,2,1:T(8,128)(2,1)} collective-permute-done((bf16[2304,3,256]{0,2,1:T(8,128)(2,1)}, bf16[2304,3,256]{0,2,1:T(8,128)(2,1)}, u32[]{:S(2)}, u32[]{:S(2)}) %collective-permute-start.5) | collective-permute-done | bytes 3538976 | tf_op jit(solution)/shard_map/ppermute | solution.py:42
  329.6 6.4 %add_add_fusion = f32[768,768]{1,0:T(8,128)} fusion(f32[768,768]{1,0:T(8,128)S(1)} %copy-done.18, f32[768,768]{1,0:T(8,128)S(1)} %fusion.73, bf16[2304,768]{0,1:T(8,128)(2,1)} %bitcast.29, bf16[768,768]{1,0:T(8,128)(2,1)S(1)} %copy-done.11, bf16[768,768]{1,0:T(8,128)(2,1)S(1)} %copy-done.14, bf16[768,768]{1,0:T(8,128)(2,1)S(1)} %copy-done.8), kind=kOutput, calls=%fused_computation.16 | convolution fusion | flops 2729705472 | bytes 14155776 | tf_op jit(solution)/shard_map/dot_general | solution.py:124
  335.9 2.9 reshape.431
  342.8 11.0 %fusion.7 = f32[3,256,3,1,128]{1,4,2,0,3:T(8,128)S(1)} fusion(bf16[6144,3,128]{0,2,1:T(8,128)(2,1)} %all-gather.11.cloned.1.call-done, bf16[3,256,6144]{2,1,0:T(8,128)(2,1)} %fusion.3), kind=kOutput, calls=%fused_computation.24 | convolution fusion | flops 3623878656 | bytes 15335424 | tf_op jit(solution)/shard_map/dot_general | solution.py:114
  354.8 2.5 collective-permute-start.6
  357.3 3.2 collective-permute-start.7
  365.5 3.5 convolution_convert_fusion
  370.3 8.8 %collective-permute-done.10 = bf16[48,3,1024]{2,0,1:T(8,128)(2,1)S(1)} collective-permute-done((bf16[48,3,1024]{2,0,1:T(8,128)(2,1)S(1)}, bf16[48,3,1024]{2,0,1:T(8,128)(2,1)S(1)}, u32[]{:S(2)}, u32[]{:S(2)}) %collective-permute-start.10) | collective-permute-done | bytes 294944 | tf_op jit(solution)/shard_map/ppermute | solution.py:148
  380.5 3.4 collective-permute-start.12
  384.0 3.4 collective-permute-start.13
  388.4 14.1 %collective-permute-done.12 = bf16[48,3,1024]{2,0,1:T(8,128)(2,1)S(1)} collective-permute-done((bf16[48,3,1024]{2,0,1:T(8,128)(2,1)S(1)}, bf16[48,3,1024]{2,0,1:T(8,128)(2,1)S(1)}, u32[]{:S(2)}, u32[]{:S(2)}) %collective-permute-start.12) | collective-permute-done | bytes 294944 | tf_op jit(solution)/shard_map/ppermute | solution.py:159
  402.5 9.1 %collective-permute-done.13 = bf16[48,3,1024]{2,0,1:T(8,128)(2,1)S(1)} collective-permute-done((bf16[48,3,1024]{2,0,1:T(8,128)(2,1)S(1)}, bf16[48,3,1024]{2,0,1:T(8,128)(2,1)S(1)}, u32[]{:S(2)}, u32[]{:S(2)}) %collective-permute-start.13) | collective-permute-done | bytes 294944 | tf_op jit(solution)/shard_map/ppermute | solution.py:159
  (184 shorter events, 64.7 us)
Async XLA Ops:
  6.5 55.0 %all-gather.5.cloned.1.call-start = ((), (), s32[]{:S(2)}) async-start(), calls=%async_computation | async-start | bytes 2949120 | tf_op jit(solution)/shard_map/all_gather | solution.py:30
  11.4 139.1 %all-gather.7.cloned.1.call-start = ((), (), s32[]{:S(2)}) async-start(), calls=%async_computation.1 | async-start | bytes 5898240 | tf_op jit(solution)/shard_map/all_gather | solution.py:30
  61.6 186.0 %all-gather.9.cloned.1.call-start = ((), (), s32[]{:S(2)}) async-start(), calls=%async_computation.2 | async-start | bytes 5898240 | tf_op jit(solution)/shard_map/all_gather | solution.py:30
  64.6 40.4 %collective-permute-start = (bf16[2304,3,128]{0,2,1:T(8,128)(2,1)}, bf16[2304,3,128]{0,2,1:T(8,128)(2,1)}, u32[]{:S(2)}, u32[]{:S(2)}) collective-permute-start(bf16[2304,3,128]{0,2,1:T(8,128)(2,1)} %pad_maximum_fusion.4), channel_id=1, source_target_pairs={{0,16},{16,0},{1,17},{17,1},{2,18},{18,2},{3,19},{19,3},{4,20},{20... | collective-permute-start | bytes 5308424 | tf_op jit(solution)/shard_map/ppermute | solution.py:42
  66.1 14.8 %collective-permute-start.4 = (s32[3]{0:T(128)S(1)}, s32[3]{0:T(128)S(1)}, u32[]{:S(2)}, u32[]{:S(2)}) collective-permute-start(s32[3]{0:T(128)S(1)} %copy-done.17), channel_id=1, source_target_pairs={{0,12},{4,0},{8,4},{12,8},{1,13},{5,1},{9,5},{13,9},{2,14},{6,2},{... | collective-permute-start | bytes 44 | tf_op jit(solution)/shard_map/ppermute | solution.py:104
  68.2 12.7 %collective-permute-start.2 = (s32[3]{0:T(128)S(1)}, s32[3]{0:T(128)S(1)}, u32[]{:S(2)}, u32[]{:S(2)}) collective-permute-start(s32[3]{0:T(128)S(1)} %copy-done.17), channel_id=1, source_target_pairs={{0,4},{4,8},{8,12},{12,0},{1,5},{5,9},{9,13},{13,1},{2,6},{6,10},{... | collective-permute-start | bytes 44 | tf_op jit(solution)/shard_map/ppermute | solution.py:104
  68.2 12.7 %collective-permute-start.3 = (s32[3]{0:T(128)S(1)}, s32[3]{0:T(128)}, u32[]{:S(2)}, u32[]{:S(2)}) collective-permute-start(s32[3]{0:T(128)S(1)} %copy-done.17), channel_id=1, source_target_pairs={{0,8},{4,12},{8,0},{12,4},{1,9},{5,13},{9,1},{13,5},{2,10},{6,14},... | collective-permute-start | bytes 44 | tf_op jit(solution)/shard_map/ppermute | solution.py:104
  80.8 29.3 %copy-start.15 = (pred[4]{0:T(512)(128)(4,1)}, pred[4]{0:T(512)(128)(4,1)S(1)}, u32[]{:S(2)}) copy-start(pred[4]{0:T(512)(128)(4,1)S(1)} %compare_and_fusion.1) | copy-start | bytes 16
  150.5 192.3 %all-gather.11.cloned.1.call-start = ((), (), s32[]{:S(2)}) async-start(), calls=%async_computation.3 | async-start | bytes 5898240 | tf_op jit(solution)/shard_map/all_gather | solution.py:77
  153.6 78.4 %collective-permute-start.1 = (bf16[2304,3,256]{0,2,1:T(8,128)(2,1)S(1)}, bf16[2304,3,256]{0,2,1:T(8,128)(2,1)}, u32[]{:S(2)}, u32[]{:S(2)}) collective-permute-start(bf16[2304,3,256]{0,2,1:T(8,128)(2,1)S(1)} %pad_maximum_fusion.1), channel_id=1, source_target_pairs={{0,16},{16,0},{1,17},{17,1},{2,18},{18,2},{3,19},{19,3},{4,20},{20... | collective-permute-start | bytes 10616840 | tf_op jit(solution)/shard_map/ppermute | solution.py:42
  167.4 6.4 %copy-start.5 = (bf16[768,3,256]{0,2,1:T(8,128)(2,1)S(1)}, bf16[768,3,256]{0,2,1:T(8,128)(2,1)}, u32[]{:S(2)}) copy-start(bf16[768,3,256]{0,2,1:T(8,128)(2,1)} %copy.179) | copy-start | bytes 3538948
  169.7 7.8 %copy-start = (bf16[3,256,6144]{2,1,0:T(8,128)(2,1)S(1)}, bf16[3,256,6144]{2,1,0:T(8,128)(2,1)}, u32[]{:S(2)}) copy-start(bf16[3,256,6144]{2,1,0:T(8,128)(2,1)} %fusion.3) | copy-start | bytes 28311556
  180.6 51.4 %copy-start.1 = (bf16[768,3072]{1,0:T(8,128)(2,1)}, bf16[768,3072]{1,0:T(8,128)(2,1)S(1)}, u32[]{:S(2)}) copy-start(bf16[768,3072]{1,0:T(8,128)(2,1)S(1)} %pad_maximum_fusion) | copy-start | bytes 14155780
  183.3 48.7 %copy-start.3 = (bf16[3072,3,128]{0,2,1:T(8,128)(2,1)S(1)}, bf16[3072,3,128]{0,2,1:T(8,128)(2,1)}, u32[]{:S(2)}) copy-start(bf16[3072,3,128]{0,2,1:T(8,128)(2,1)} %all-gather.5.cloned.1.call-done) | copy-start | bytes 7077892
  249.8 3.5 copy-start.7
  249.9 4.0 copy-start.19
  251.8 77.7 %collective-permute-start.5 = (bf16[2304,3,256]{0,2,1:T(8,128)(2,1)}, bf16[2304,3,256]{0,2,1:T(8,128)(2,1)}, u32[]{:S(2)}, u32[]{:S(2)}) collective-permute-start(bf16[2304,3,256]{0,2,1:T(8,128)(2,1)} %pad_maximum_fusion.3), channel_id=1, source_target_pairs={{0,16},{16,0},{1,17},{17,1},{2,18},{18,2},{3,19},{19,3},{4,20},{20... | collective-permute-start | bytes 10616840 | tf_op jit(solution)/shard_map/ppermute | solution.py:42
  267.4 62.1 %copy-start.8 = (bf16[768,768]{1,0:T(8,128)(2,1)S(1)}, bf16[768,768]{1,0:T(8,128)(2,1)}, u32[]{:S(2)}) copy-start(bf16[768,768]{1,0:T(8,128)(2,1)} %copy-done.6) | copy-start | bytes 3538948
  267.4 62.1 %copy-start.11 = (bf16[768,768]{1,0:T(8,128)(2,1)S(1)}, bf16[768,768]{1,0:T(8,128)(2,1)}, u32[]{:S(2)}) copy-start(bf16[768,768]{1,0:T(8,128)(2,1)} %get-tuple-element.38) | copy-start | bytes 3538948
  267.4 62.1 %copy-start.14 = (bf16[768,768]{1,0:T(8,128)(2,1)S(1)}, bf16[768,768]{1,0:T(8,128)(2,1)}, u32[]{:S(2)}) copy-start(bf16[768,768]{1,0:T(8,128)(2,1)} %get-tuple-element.39) | copy-start | bytes 3538948
  267.5 62.1 %copy-start.18 = (f32[768,768]{1,0:T(8,128)S(1)}, f32[768,768]{1,0:T(8,128)}, u32[]{:S(2)}) copy-start(f32[768,768]{1,0:T(8,128)} %fusion.20) | copy-start | bytes 7077892
  354.2 6.3 %copy-start.16 = (pred[4]{0:T(512)(128)(4,1)S(1)}, pred[4]{0:T(512)(128)(4,1)}, u32[]{:S(2)}) copy-start(pred[4]{0:T(512)(128)(4,1)} %copy-done.15) | copy-start | bytes 16
  354.8 6.5 %collective-permute-start.6 = (bf16[48,768]{1,0:T(8,128)(2,1)S(1)}, bf16[48,768]{1,0:T(8,128)(2,1)S(1)}, u32[]{:S(2)}, u32[]{:S(2)}) collective-permute-start(bf16[48,768]{1,0:T(8,128)(2,1)S(1)} %get-tuple-element.73), channel_id=1, source_target_pairs={{0,4},{4,8},{8,12},{12,0},{1,5},{5,9},{9,13},{13,1},{2,6},{6,10},{... | collective-permute-start | bytes 221192 | tf_op jit(solution)/shard_map/ppermute | solution.py:132
  357.3 6.4 %collective-permute-start.7 = (bf16[48,768]{1,0:T(8,128)(2,1)S(1)}, bf16[48,768]{1,0:T(8,128)(2,1)S(1)}, u32[]{:S(2)}, u32[]{:S(2)}) collective-permute-start(bf16[48,768]{1,0:T(8,128)(2,1)S(1)} %get-tuple-element.73), channel_id=1, source_target_pairs={{0,8},{4,12},{8,0},{12,4},{1,9},{5,13},{9,1},{13,5},{2,10},{6,14},... | collective-permute-start | bytes 221192 | tf_op jit(solution)/shard_map/ppermute | solution.py:132
  360.5 4.4 %collective-permute-start.8 = (bf16[48,768]{1,0:T(8,128)(2,1)S(1)}, bf16[48,768]{1,0:T(8,128)(2,1)S(1)}, u32[]{:S(2)}, u32[]{:S(2)}) collective-permute-start(bf16[48,768]{1,0:T(8,128)(2,1)S(1)} %get-tuple-element.73), channel_id=1, source_target_pairs={{0,12},{4,0},{8,4},{12,8},{1,13},{5,1},{9,5},{13,9},{2,14},{6,2},{... | collective-permute-start | bytes 221192 | tf_op jit(solution)/shard_map/ppermute | solution.py:132
  369.1 9.9 %collective-permute-start.10 = (bf16[48,3,1024]{2,0,1:T(8,128)(2,1)S(1)}, bf16[48,3,1024]{2,0,1:T(8,128)(2,1)S(1)}, u32[]{:S(2)}, u32[]{:S(2)}) collective-permute-start(bf16[48,3,1024]{2,0,1:T(8,128)(2,1)S(1)} %get-tuple-element.69), channel_id=1, source_target_pairs={{0,2},{1,3},{2,0},{3,1},{4,6},{5,7},{6,4},{7,5},{8,10},{9,11},{10,... | collective-permute-start | bytes 884744 | tf_op jit(solution)/shard_map/ppermute | solution.py:148
  369.7 10.6 %collective-permute-start.11 = (bf16[48,3,1024]{2,0,1:T(8,128)(2,1)S(1)}, bf16[48,3,1024]{2,0,1:T(8,128)(2,1)S(1)}, u32[]{:S(2)}, u32[]{:S(2)}) collective-permute-start(bf16[48,3,1024]{2,0,1:T(8,128)(2,1)S(1)} %get-tuple-element.68), channel_id=1, source_target_pairs={{0,3},{1,0},{2,1},{3,2},{4,7},{5,4},{6,5},{7,6},{8,11},{9,8},{10,9... | collective-permute-start | bytes 884744 | tf_op jit(solution)/shard_map/ppermute | solution.py:148
  369.7 10.6 %collective-permute-start.9 = (bf16[48,3,1024]{2,0,1:T(8,128)(2,1)S(1)}, bf16[48,3,1024]{2,0,1:T(8,128)(2,1)S(1)}, u32[]{:S(2)}, u32[]{:S(2)}) collective-permute-start(bf16[48,3,1024]{2,0,1:T(8,128)(2,1)S(1)} %get-tuple-element.67), channel_id=1, source_target_pairs={{0,1},{1,2},{2,3},{3,0},{4,5},{5,6},{6,7},{7,4},{8,9},{9,10},{10,1... | collective-permute-start | bytes 884744 | tf_op jit(solution)/shard_map/ppermute | solution.py:148
  380.5 21.9 %collective-permute-start.12 = (bf16[48,3,1024]{2,0,1:T(8,128)(2,1)S(1)}, bf16[48,3,1024]{2,0,1:T(8,128)(2,1)S(1)}, u32[]{:S(2)}, u32[]{:S(2)}) collective-permute-start(bf16[48,3,1024]{2,0,1:T(8,128)(2,1)S(1)} %add_convert_fusion), channel_id=1, source_target_pairs={{0,0},{1,4},{2,8},{3,12},{4,1},{5,5},{6,9},{7,13},{8,2},{9,6},{10,... | collective-permute-start | bytes 884744 | tf_op jit(solution)/shard_map/ppermute | solution.py:159
  384.0 27.6 %collective-permute-start.13 = (bf16[48,3,1024]{2,0,1:T(8,128)(2,1)S(1)}, bf16[48,3,1024]{2,0,1:T(8,128)(2,1)S(1)}, u32[]{:S(2)}, u32[]{:S(2)}) collective-permute-start(bf16[48,3,1024]{2,0,1:T(8,128)(2,1)S(1)} %add_convert_fusion), channel_id=1, source_target_pairs={{0,4},{1,8},{2,12},{3,0},{4,5},{5,9},{6,13},{7,1},{8,6},{9,10},{10... | collective-permute-start | bytes 884744 | tf_op jit(solution)/shard_map/ppermute | solution.py:159
  387.4 24.2 %collective-permute-start.14 = (bf16[48,3,1024]{2,0,1:T(8,128)(2,1)S(1)}, bf16[48,3,1024]{2,0,1:T(8,128)(2,1)S(1)}, u32[]{:S(2)}, u32[]{:S(2)}) collective-permute-start(bf16[48,3,1024]{2,0,1:T(8,128)(2,1)S(1)} %add_convert_fusion), channel_id=1, source_target_pairs={{0,8},{1,12},{2,0},{3,4},{4,9},{5,13},{6,1},{7,5},{8,10},{9,14},{1... | collective-permute-start | bytes 884744 | tf_op jit(solution)/shard_map/ppermute | solution.py:159
  387.6 25.2 %collective-permute-start.15 = (bf16[48,3,1024]{2,0,1:T(8,128)(2,1)S(1)}, bf16[48,3,1024]{2,0,1:T(8,128)(2,1)S(1)}, u32[]{:S(2)}, u32[]{:S(2)}) collective-permute-start(bf16[48,3,1024]{2,0,1:T(8,128)(2,1)S(1)} %add_convert_fusion), channel_id=1, source_target_pairs={{0,12},{1,0},{2,4},{3,8},{4,13},{5,1},{6,5},{7,9},{8,14},{9,2},{10... | collective-permute-start | bytes 884744 | tf_op jit(solution)/shard_map/ppermute | solution.py:159
  (8 other events, 20.0 us)
Sparse Core Ops, SparseCore 0:
  11.5 50.0 all-gather.4
  63.1 87.2 all-gather.6
  152.0 87.8 all-gather.8
  247.7 87.9 all-gather.10
where the time goes:
time: 431 us; the launch traced here: 424 us
  waiting for transfers between devices  239 us (55%)
  matrix products  63.5 us (15%)
  local copies, waits for them, and re-layouts  45.9 us (11%)
  other arithmetic  36.9 us (9%)
  starting transfers between devices  24.5 us (6%)
  between operations  14.3 us (3%)
    ppermute x3, waiting for transfers between devices, forward(): return lax.ppermute(onward, 'groups', [(0, 1), (1, 0)])  123 us
    all_gather x3, waiting for transfers between devices, moved_weights(): gathered = lax.all_gather(mine, 'video', axis=0, tiled=True)  77.6 us
    ppermute x4, waiting for transfers between devices, per_device(): got = lax.ppermute(clip_rows, ('video', 'tensor'), pairs)  24.4 us
    dot_general x3, matrix products, per_device(): jnp.dot(own_half, gathered.reshape(n_video * half, width), preferred_elem...  17.3 us
    dot_general x3, matrix products, per_device(): jnp.dot(rolled, received.reshape((n_video - 1) * half, width), preferred_...  16.6 us
    convert_element_type x1, other arithmetic, per_device(): normed = normed.astype(jnp.bfloat16).reshape(patch_rows, frames.shape[2])  12.2 us
    unnamed x55, local copies, waits for them, and re-layouts  11.3 us
    dot_general x1, matrix products, per_device(): proj = jnp.dot(normed, full, preferred_element_type=jnp.float32)  11 us
  transfers between devices with their start and end apart: 20, of which 13 were waited for; matrix products, arithmetic and copies ran while one was open for 28% of the time, Pallas kernels for 0%

commit v1 on v0

--- a/solution.py
+++ b/solution.py
@@ -27,7 +27,22 @@
     if after is not None:
         mine, after = lax.optimization_barrier((mine, after))
     other = lax.dynamic_slice_in_dim(chunk, (1 - g) * half, half, axis=0)
-    gathered = lax.all_gather(mine, "video", axis=0, tiled=True)
+
+    def cut_tasks(block_in, shard_axis):
+        axis_len = lax.axis_size(shard_axis)
+        table = tuple(((dev_j, (dev_j + 1) % axis_len) for dev_j in range(axis_len)))
+        block_next, u1 = ([block_in], [block_in])
+        copies = tuple(((dev_j, (dev_j - 1) % axis_len) for dev_j in range(axis_len)))
+        for _ in range(axis_len // 2):
+            block_next.append(lax.ppermute(block_next[-1], shard_axis, perm=table))
+        for _ in range((axis_len - 1) // 2):
+            u1.append(lax.ppermute(u1[-1], shard_axis, copies))
+        frame_out = jnp.concatenate([*block_next[::-1], *u1[1:]], 0)
+        return jnp.roll(
+            frame_out, (lax.axis_index(shard_axis) - axis_len // 2) * block_in.shape[0], axis=0
+        )
+
+    gathered = cut_tasks(mine, "video")
     onward = jnp.concatenate(
         [
             lax.dynamic_slice_in_dim(gathered, (v + 1 + i) % n_video * half, half, axis=0)

time: 431 us -> 448 us (1.039)
  waiting for transfers between devices: 239 us -> 192 us
  local copies, waits for them, and re-layouts: 45.9 us -> 67.5 us
  starting transfers between devices: 24.5 us -> 44 us
  other arithmetic: 36.9 us -> 52.6 us
  matrix products: 63.5 us -> 70.6 us
    ppermute x0 -> x9, waiting for transfers between devices: none -> 90.7 us  [the longest x6 90.7 us: cut_tasks(): block_next.append(lax.ppermute(block_next[-1], shard_axis, perm=table))]
    all_gather x3 -> x0, waiting for transfers between devices: 77.6 us -> none  [moved_weights(): gathered = lax.all_gather(mine, 'video', axis=0, tiled=True)]
    ppermute x3, waiting for transfers between devices: 123 us -> 50.6 us  [forward(): return lax.ppermute(onward, 'groups', [(0, 1), (1, 0)])]
    ppermute x0 -> x9, starting transfers between devices: none -> 22.8 us  [the longest x6 19.5 us: cut_tasks(): block_next.append(lax.ppermute(block_next[-1], shard_axis, perm=table))]
    dynamic_slice x0 -> x3, local copies, waits for them, and re-layouts: none -> 13.9 us  [cut_tasks(): jnp.roll(frame_out, (lax.axis_index(shard_axis) - axis_len // 2) * block_...]
    concatenate x0 -> x2, other arithmetic: none -> 10.1 us  [cut_tasks(): jnp.roll(frame_out, (lax.axis_index(shard_axis) - axis_len // 2) * block_...]
    ppermute x3, waiting for transfers between devices: 0.01 us -> 9.31 us  [per_device(): lax.ppermute(frame_video, 'video', [(a, (a + k) % n_video) for a in range...]
    dot_general x3, matrix products: 17.3 us -> 22.7 us  [per_device(): jnp.dot(own_half, gathered.reshape(n_video * half, width), preferred_elem...]
  transfers between devices with their start and end apart: 20 -> 26, of which waited for: 13 -> 18; matrix products, arithmetic and copies ran while one was open for 28% -> 33% of each run, Pallas kernels for 0% -> 0%
where the time goes in v1:
time: 448 us; the launch traced here: 442 us
  waiting for transfers between devices  192 us (43%)
  matrix products  70.6 us (16%)
  local copies, waits for them, and re-layouts  67.5 us (15%)
  other arithmetic  52.6 us (12%)
  starting transfers between devices  44 us (10%)
  between operations  14.5 us (3%)
    ppermute x6, waiting for transfers between devices, cut_tasks(): block_next.append(lax.ppermute(block_next[-1], shard_axis, perm=table))  90.7 us
    ppermute x3, waiting for transfers between devices, forward(): return lax.ppermute(onward, 'groups', [(0, 1), (1, 0)])  50.6 us
    ppermute x4, waiting for transfers between devices, per_device(): got = lax.ppermute(clip_rows, ('video', 'tensor'), pairs)  25.4 us
    dot_general x3, matrix products, per_device(): jnp.dot(own_half, gathered.reshape(n_video * half, width), preferred_elem...  22.7 us
    dot_general x3, matrix products, per_device(): jnp.dot(rolled, received.reshape((n_video - 1) * half, width), preferred_...  19.7 us
    ppermute x6, starting transfers between devices, cut_tasks(): block_next.append(lax.ppermute(block_next[-1], shard_axis, perm=table))  19.5 us
    unnamed x62, local copies, waits for them, and re-layouts  14 us
    dynamic_slice x3, local copies, waits for them, and re-layouts, cut_tasks(): jnp.roll(frame_out, (lax.axis_index(shard_axis) - axis_len // 2) * block_...  13.9 us
  transfers between devices with their start and end apart: 26, of which 18 were waited for; matrix products, arithmetic and copies ran while one was open for 33% of the time, Pallas kernels for 0%

profile of v1, /device:TPU:10, one launch (start us, length us, event | category | flops | bytes accessed | tf_op | source)
XLA Modules:
  0.0 441.6 jit_solution(2055930263515296257)
XLA Ops:
  12.6 14.3 %collective-permute-done = bf16[768,3,128]{0,2,1:T(8,128)(2,1)} collective-permute-done((bf16[768,3,128]{0,2,1:T(8,128)(2,1)S(1)}, bf16[768,3,128]{0,2,1:T(8,128)(2,1)}, u32[]{:S(2)}, u32[]{:S(2)}) %collective-permute-start) | collective-permute-done | bytes 589856 | tf_op jit(solution)/shard_map/ppermute | solution.py:37
  26.9 12.0 %collective-permute-start.1 = (bf16[768,3,128]{0,2,1:T(8,128)(2,1)}, bf16[768,3,128]{0,2,1:T(8,128)(2,1)}, u32[]{:S(2)}, u32[]{:S(2)}) collective-permute-start(bf16[768,3,128]{0,2,1:T(8,128)(2,1)} %collective-permute-done), channel_id=1, source_target_pairs={{0,4},{4,8},{8,12},{12,0},{1,5},{5,9},{9,13},{13,1},{2,6},{6,10},{... | collective-permute-start | bytes 1769480 | tf_op jit(solution)/shard_map/ppermute | solution.py:37
  38.9 4.1 fusion.68
  43.0 8.1 %collective-permute-done.1 = bf16[768,3,128]{0,2,1:T(8,128)(2,1)} collective-permute-done((bf16[768,3,128]{0,2,1:T(8,128)(2,1)}, bf16[768,3,128]{0,2,1:T(8,128)(2,1)}, u32[]{:S(2)}, u32[]{:S(2)}) %collective-permute-start.1) | collective-permute-done | bytes 589856 | tf_op jit(solution)/shard_map/ppermute | solution.py:37
  65.9 4.1 constant_dynamic-slice_fusion.21
  73.6 5.0 %collective-permute-start.9 = (s32[3]{0:T(128)S(1)}, s32[3]{0:T(128)S(1)}, u32[]{:S(2)}, u32[]{:S(2)}) collective-permute-start(s32[3]{0:T(128)S(1)} %copy-done.15), channel_id=1, source_target_pairs={{0,8},{4,12},{8,0},{12,4},{1,9},{5,13},{9,1},{13,5},{2,10},{6,14},... | collective-permute-start | bytes 44 | tf_op jit(solution)/shard_map/ppermute | solution.py:119
  88.5 8.2 %collective-permute-done.8 = s32[3]{0:T(128)S(1)} collective-permute-done((s32[3]{0:T(128)S(1)}, s32[3]{0:T(128)S(1)}, u32[]{:S(2)}, u32[]{:S(2)}) %collective-permute-start.8) | collective-permute-done | bytes 44 | tf_op jit(solution)/shard_map/ppermute | solution.py:119
  100.7 5.0 %convert_reduce_fusion = f32[3,256]{1,0:T(4,128)S(1)} fusion(bf16[3,256,6144]{2,1,0:T(8,128)(2,1)} %param.6), kind=kLoop, calls=%fused_computation.4 | loop fusion | flops 9436416 | bytes 9440256 | tf_op jit(solution)/shard_map/reduce_sum | solution.py:102
  105.7 6.3 %fusion.2 = f32[3,256]{1,0:T(4,128)S(1)} fusion(bf16[3,256,6144]{2,1,0:T(8,128)(2,1)} %param.6, f32[3,256]{1,0:T(4,128)S(1)} %broadcast_multiply_fusion), kind=kLoop, calls=%fused_computation.7 | loop fusion | flops 18873600 | bytes 9443328 | tf_op jit(solution)/shard_map/reduce_sum | solution.py:103
  112.0 12.2 %fusion.3 = bf16[3,256,6144]{2,1,0:T(8,128)(2,1)} fusion(bf16[3,256,6144]{2,1,0:T(8,128)(2,1)} %param.6, f32[3,256]{1,0:T(4,128)S(1)} %add_rsqrt_fusion.10, f32[3,256]{1,0:T(4,128)S(1)} %broadcast_multiply_fusion), kind=kLoop, calls=%fused_computation.8 | loop fusion | flops 18874368 | bytes 18880512 | tf_op jit(solution)/shard_map/convert_element_type | solution.py:104
  124.2 4.1 fusion.22
  129.4 20.2 %collective-permute-done.5 = bf16[768,3,256]{0,2,1:T(8,128)(2,1)} collective-permute-done((bf16[768,3,256]{0,2,1:T(8,128)(2,1)}, bf16[768,3,256]{0,2,1:T(8,128)(2,1)}, u32[]{:S(2)}, u32[]{:S(2)}) %collective-permute-start.5) | collective-permute-done | bytes 1179680 | tf_op jit(solution)/shard_map/ppermute | solution.py:37
  149.6 6.2 %maximum_maximum_fusion = bf16[6144,3,256]{0,2,1:T(8,128)(2,1)S(1)} fusion(bf16[768,3,256]{0,2,1:T(8,128)(2,1)} %copy-done.6, bf16[768,3,256]{0,2,1:T(8,128)(2,1)S(1)} %copy.173, bf16[768,3,256]{0,2,1:T(8,128)(2,1)} %collective-permute-done.4, bf16[768,3,256]{0,2,1:T(8,128)(2,1)} %collective-permute-done.5), kind=kLoop, calls=%fused_computation.9 | loop fusion | flops 75497472 | bytes 14155776 | tf_op jit(solution)/shard_map/jit(_roll_dynamic)/concatenate | solution.py:41
  155.8 4.9 %constant_dynamic-slice_fusion.8 = bf16[3072,3,256]{0,2,1:T(8,128)(2,1)} fusion(bf16[6144,3,256]{0,2,1:T(8,128)(2,1)S(1)} %maximum_maximum_fusion, s32[]{:T(128)S(6)} %select_n.222), kind=kLoop, calls=%fused_computation.139 | loop fusion | bytes 9437188 | tf_op jit(solution)/shard_map/jit(_roll_dynamic)/dynamic_slice | solution.py:41
  167.5 5.5 %pad_maximum_fusion = bf16[768,3072]{1,0:T(8,128)(2,1)} fusion(bf16[768,768]{1,0:T(8,128)(2,1)} %get-tuple-element.41, bf16[768,768]{1,0:T(8,128)(2,1)} %get-tuple-element.42, bf16[768,768]{1,0:T(8,128)(2,1)} %get-tuple-element.43, bf16[768,768]{1,0:T(8,128)(2,1)} %get-tuple-element.44), kind=kLoop, calls=%fused_computation.13 | loop fusion | flops 18874368 | bytes 9437184 | tf_op jit(solution)/shard_map/concatenate | solution.py:111
  176.4 33.6 %collective-permute-done.11 = bf16[768,3,256]{0,2,1:T(8,128)(2,1)} collective-permute-done((bf16[768,3,256]{0,2,1:T(8,128)(2,1)S(1)}, bf16[768,3,256]{0,2,1:T(8,128)(2,1)}, u32[]{:S(2)}, u32[]{:S(2)}) %collective-permute-start.11) | collective-permute-done | bytes 1179680 | tf_op jit(solution)/shard_map/ppermute | solution.py:37
  217.7 4.5 %fusion.65 = f32[768,384]{1,0:T(8,128)} fusion(bf16[2304,384]{0,1:T(8,128)(2,1)} %bitcast.11, bf16[768,768]{1,0:T(8,128)(2,1)S(1)} %copy-done.11, bf16[768,768]{1,0:T(8,128)(2,1)S(1)} %copy-done.13, bf16[768,768]{1,0:T(8,128)(2,1)S(1)} %copy-done.9), kind=kOutput, calls=%fused_computation.186 | convolution fusion | flops 1369571328 | bytes 6488064 | tf_op jit(solution)/shard_map/dot_general | solution.py:139
  222.2 14.5 %collective-permute-done.12 = bf16[768,3,256]{0,2,1:T(8,128)(2,1)S(1)} collective-permute-done((bf16[768,3,256]{0,2,1:T(8,128)(2,1)}, bf16[768,3,256]{0,2,1:T(8,128)(2,1)S(1)}, u32[]{:S(2)}, u32[]{:S(2)}) %collective-permute-start.12) | collective-permute-done | bytes 1179680 | tf_op jit(solution)/shard_map/ppermute | solution.py:37
  236.7 3.9 maximum_maximum_fusion.1
  245.0 4.9 %constant_dynamic-slice_fusion.19 = bf16[3072,3,256]{0,2,1:T(8,128)(2,1)} fusion(bf16[6144,3,256]{0,2,1:T(8,128)(2,1)S(1)} %maximum_maximum_fusion.1, s32[]{:T(128)S(6)} %select_n.222), kind=kLoop, calls=%fused_computation.150 | loop fusion | bytes 9437188 | tf_op jit(solution)/shard_map/jit(_roll_dynamic)/dynamic_slice | solution.py:41
  249.9 45.2 %collective-permute-done.7 = bf16[2304,3,256]{0,2,1:T(8,128)(2,1)} collective-permute-done((bf16[2304,3,256]{0,2,1:T(8,128)(2,1)}, bf16[2304,3,256]{0,2,1:T(8,128)(2,1)}, u32[]{:S(2)}, u32[]{:S(2)}) %collective-permute-start.7) | collective-permute-done | bytes 3538976 | tf_op jit(solution)/shard_map/ppermute | solution.py:57
  295.2 6.4 %fusion.12 = f32[768,384]{1,0:T(8,128)} fusion(f32[768,384]{1,0:T(8,128)} %fusion.65, f32[768,384]{1,0:T(8,128)S(1)} %copy-done.7, bf16[768,3072]{1,0:T(8,128)(2,1)} %pad_maximum_fusion, bf16[3072,384]{0,1:T(8,128)(2,1)S(1)} %bitcast.195), kind=kOutput, calls=%fused_computation.28 | convolution fusion | flops 1812529152 | bytes 10616832 | tf_op jit(solution)/shard_map/dot_general | solution.py:136
  307.1 9.0 %fusion.72 = f32[768,768]{1,0:T(8,128)} fusion(bf16[768,3072]{1,0:T(8,128)(2,1)} %pad_maximum_fusion, bf16[3072,768]{0,1:T(8,128)(2,1)} %bitcast.191), kind=kOutput, calls=%fused_computation.193 | convolution fusion | flops 3623878656 | bytes 11796480 | tf_op jit(solution)/shard_map/dot_general | solution.py:136
  317.8 8.8 %add_add_fusion.1 = f32[768,768]{1,0:T(8,128)} fusion(f32[768,768]{1,0:T(8,128)} %fusion.22, f32[768,768]{1,0:T(8,128)} %fusion.72, bf16[2304,768]{0,1:T(8,128)(2,1)} %bitcast.21, bf16[768,768]{1,0:T(8,128)(2,1)} %get-tuple-element.39, bf16[768,768]{1,0:T(8,128)(2,1)} %get-tuple-element.40, bf16[768,768]{1,0:T(8,128)(2,1)} %get-tuple-element.38), kind=kOutput, calls=%fused_computation.19 | convolution fusion | flops 2729705472 | bytes 14155776 | tf_op jit(solution)/shard_map/dot_general | solution.py:139
  333.8 7.3 %fusion.73 = f32[768,768]{1,0:T(8,128)S(1)} fusion(bf16[768,3072]{1,0:T(8,128)(2,1)} %pad_maximum_fusion, bf16[3072,768]{0,1:T(8,128)(2,1)} %bitcast.192), kind=kOutput, calls=%fused_computation.194 | convolution fusion | flops 3623878656 | bytes 11796480 | tf_op jit(solution)/shard_map/dot_general | solution.py:136
  341.0 5.3 %collective-permute-done.14 = bf16[2304,3,256]{0,2,1:T(8,128)(2,1)} collective-permute-done((bf16[2304,3,256]{0,2,1:T(8,128)(2,1)}, bf16[2304,3,256]{0,2,1:T(8,128)(2,1)}, u32[]{:S(2)}, u32[]{:S(2)}) %collective-permute-start.14) | collective-permute-done | bytes 3538976 | tf_op jit(solution)/shard_map/ppermute | solution.py:57
  346.4 6.4 %add_add_fusion = f32[768,768]{1,0:T(8,128)} fusion(f32[768,768]{1,0:T(8,128)S(1)} %copy-done.16, f32[768,768]{1,0:T(8,128)S(1)} %fusion.73, bf16[2304,768]{0,1:T(8,128)(2,1)} %bitcast.29, bf16[768,768]{1,0:T(8,128)(2,1)S(1)} %copy-done.12, bf16[768,768]{1,0:T(8,128)(2,1)S(1)} %copy-done.14, bf16[768,768]{1,0:T(8,128)(2,1)S(1)} %copy-done.10), kind=kOutput, calls=%fused_computation.18 | convolution fusion | flops 2729705472 | bytes 14155776 | tf_op jit(solution)/shard_map/dot_general | solution.py:139
  359.7 11.0 %fusion.7 = f32[3,256,3,1,128]{1,4,2,0,3:T(8,128)S(1)} fusion(bf16[6144,3,128]{0,2,1:T(8,128)(2,1)} %all-gather.2.cloned.1.call-done, bf16[3,256,6144]{2,1,0:T(8,128)(2,1)} %fusion.3), kind=kOutput, calls=%fused_computation.26 | convolution fusion | flops 3623878656 | bytes 15335424 | tf_op jit(solution)/shard_map/dot_general | solution.py:129
  385.3 6.7 %collective-permute-done.18 = bf16[48,3,1024]{2,0,1:T(8,128)(2,1)S(1)} collective-permute-done((bf16[48,3,1024]{2,0,1:T(8,128)(2,1)S(1)}, bf16[48,3,1024]{2,0,1:T(8,128)(2,1)S(1)}, u32[]{:S(2)}, u32[]{:S(2)}) %collective-permute-start.18) | collective-permute-done | bytes 294944 | tf_op jit(solution)/shard_map/ppermute | solution.py:163
  397.2 4.2 collective-permute-start.21
  404.8 14.1 %collective-permute-done.21 = bf16[48,3,1024]{2,0,1:T(8,128)(2,1)S(1)} collective-permute-done((bf16[48,3,1024]{2,0,1:T(8,128)(2,1)S(1)}, bf16[48,3,1024]{2,0,1:T(8,128)(2,1)S(1)}, u32[]{:S(2)}, u32[]{:S(2)}) %collective-permute-start.21) | collective-permute-done | bytes 294944 | tf_op jit(solution)/shard_map/ppermute | solution.py:174
  418.9 9.3 %collective-permute-done.22 = bf16[48,3,1024]{2,0,1:T(8,128)(2,1)S(1)} collective-permute-done((bf16[48,3,1024]{2,0,1:T(8,128)(2,1)S(1)}, bf16[48,3,1024]{2,0,1:T(8,128)(2,1)S(1)}, u32[]{:S(2)}, u32[]{:S(2)}) %collective-permute-start.22) | collective-permute-done | bytes 294944 | tf_op jit(solution)/shard_map/ppermute | solution.py:174
  (207 shorter events, 111.8 us)
Async XLA Ops:
  6.5 353.2 %all-gather.2.cloned.1.call-start = ((), (), s32[]{:S(2)}) async-start(), calls=%async_computation | async-start | bytes 5898240 | tf_op jit(solution)/shard_map/all_gather | solution.py:92
  10.5 16.4 %collective-permute-start = (bf16[768,3,128]{0,2,1:T(8,128)(2,1)S(1)}, bf16[768,3,128]{0,2,1:T(8,128)(2,1)}, u32[]{:S(2)}, u32[]{:S(2)}) collective-permute-start(bf16[768,3,128]{0,2,1:T(8,128)(2,1)S(1)} %copy.170), channel_id=1, source_target_pairs={{0,4},{4,8},{8,12},{12,0},{1,5},{5,9},{9,13},{13,1},{2,6},{6,10},{... | collective-permute-start | bytes 1769480 | tf_op jit(solution)/shard_map/ppermute | solution.py:37
  12.1 41.3 %collective-permute-start.2 = (bf16[768,3,128]{0,2,1:T(8,128)(2,1)S(1)}, bf16[768,3,128]{0,2,1:T(8,128)(2,1)S(1)}, u32[]{:S(2)}, u32[]{:S(2)}) collective-permute-start(bf16[768,3,128]{0,2,1:T(8,128)(2,1)S(1)} %copy.170), channel_id=1, source_target_pairs={{0,12},{4,0},{8,4},{12,8},{1,13},{5,1},{9,5},{13,9},{2,14},{6,2},{... | collective-permute-start | bytes 1769480 | tf_op jit(solution)/shard_map/ppermute | solution.py:39
  26.9 24.2 %collective-permute-start.1 = (bf16[768,3,128]{0,2,1:T(8,128)(2,1)}, bf16[768,3,128]{0,2,1:T(8,128)(2,1)}, u32[]{:S(2)}, u32[]{:S(2)}) collective-permute-start(bf16[768,3,128]{0,2,1:T(8,128)(2,1)} %collective-permute-done), channel_id=1, source_target_pairs={{0,4},{4,8},{8,12},{12,0},{1,5},{5,9},{9,13},{13,1},{2,6},{6,10},{... | collective-permute-start | bytes 1769480 | tf_op jit(solution)/shard_map/ppermute | solution.py:37
  60.4 40.2 %collective-permute-start.3 = (bf16[2304,3,128]{0,2,1:T(8,128)(2,1)}, bf16[2304,3,128]{0,2,1:T(8,128)(2,1)}, u32[]{:S(2)}, u32[]{:S(2)}) collective-permute-start(bf16[2304,3,128]{0,2,1:T(8,128)(2,1)} %pad_maximum_fusion.4), channel_id=1, source_target_pairs={{0,16},{16,0},{1,17},{17,1},{2,18},{18,2},{3,19},{19,3},{4,20},{20... | collective-permute-start | bytes 5308424 | tf_op jit(solution)/shard_map/ppermute | solution.py:57
  64.3 14.2 %copy-start.5 = (bf16[768,3,128]{2,0,1:T(8,128)(2,1)S(1)}, bf16[768,3,128]{2,0,1:T(8,128)(2,1)}, u32[]{:S(2)}) copy-start(bf16[768,3,128]{2,0,1:T(8,128)(2,1)} %get-tuple-element.71) | copy-start | bytes 1769476
  70.0 30.1 %collective-permute-start.4 = (bf16[768,3,256]{0,2,1:T(8,128)(2,1)S(1)}, bf16[768,3,256]{0,2,1:T(8,128)(2,1)}, u32[]{:S(2)}, u32[]{:S(2)}) collective-permute-start(bf16[768,3,256]{0,2,1:T(8,128)(2,1)S(1)} %copy.173), channel_id=1, source_target_pairs={{0,4},{4,8},{8,12},{12,0},{1,5},{5,9},{9,13},{13,1},{2,6},{6,10},{... | collective-permute-start | bytes 3538952 | tf_op jit(solution)/shard_map/ppermute | solution.py:37
  71.5 16.9 %collective-permute-start.10 = (s32[3]{0:T(128)S(1)}, s32[3]{0:T(128)S(1)}, u32[]{:S(2)}, u32[]{:S(2)}) collective-permute-start(s32[3]{0:T(128)S(1)} %copy-done.15), channel_id=1, source_target_pairs={{0,12},{4,0},{8,4},{12,8},{1,13},{5,1},{9,5},{13,9},{2,14},{6,2},{... | collective-permute-start | bytes 44 | tf_op jit(solution)/shard_map/ppermute | solution.py:119
  72.3 24.4 %collective-permute-start.8 = (s32[3]{0:T(128)S(1)}, s32[3]{0:T(128)S(1)}, u32[]{:S(2)}, u32[]{:S(2)}) collective-permute-start(s32[3]{0:T(128)S(1)} %copy-done.15), channel_id=1, source_target_pairs={{0,4},{4,8},{8,12},{12,0},{1,5},{5,9},{9,13},{13,1},{2,6},{6,10},{... | collective-permute-start | bytes 44 | tf_op jit(solution)/shard_map/ppermute | solution.py:119
  73.6 24.2 %collective-permute-start.9 = (s32[3]{0:T(128)S(1)}, s32[3]{0:T(128)S(1)}, u32[]{:S(2)}, u32[]{:S(2)}) collective-permute-start(s32[3]{0:T(128)S(1)} %copy-done.15), channel_id=1, source_target_pairs={{0,8},{4,12},{8,0},{12,4},{1,9},{5,13},{9,1},{13,5},{2,10},{6,14},... | collective-permute-start | bytes 44 | tf_op jit(solution)/shard_map/ppermute | solution.py:119
  98.5 29.8 %collective-permute-start.6 = (bf16[768,3,256]{0,2,1:T(8,128)(2,1)S(1)}, bf16[768,3,256]{0,2,1:T(8,128)(2,1)S(1)}, u32[]{:S(2)}, u32[]{:S(2)}) collective-permute-start(bf16[768,3,256]{0,2,1:T(8,128)(2,1)S(1)} %copy.173), channel_id=1, source_target_pairs={{0,12},{4,0},{8,4},{12,8},{1,13},{5,1},{9,5},{13,9},{2,14},{6,2},{... | collective-permute-start | bytes 3538952 | tf_op jit(solution)/shard_map/ppermute | solution.py:39
  100.1 49.5 %collective-permute-start.5 = (bf16[768,3,256]{0,2,1:T(8,128)(2,1)}, bf16[768,3,256]{0,2,1:T(8,128)(2,1)}, u32[]{:S(2)}, u32[]{:S(2)}) collective-permute-start(bf16[768,3,256]{0,2,1:T(8,128)(2,1)} %collective-permute-done.4), channel_id=1, source_target_pairs={{0,4},{4,8},{8,12},{12,0},{1,5},{5,9},{9,13},{13,1},{2,6},{6,10},{... | collective-permute-start | bytes 3538952 | tf_op jit(solution)/shard_map/ppermute | solution.py:37
  160.7 49.3 %collective-permute-start.11 = (bf16[768,3,256]{0,2,1:T(8,128)(2,1)S(1)}, bf16[768,3,256]{0,2,1:T(8,128)(2,1)}, u32[]{:S(2)}, u32[]{:S(2)}) collective-permute-start(bf16[768,3,256]{0,2,1:T(8,128)(2,1)S(1)} %copy-done.1), channel_id=1, source_target_pairs={{0,4},{4,8},{8,12},{12,0},{1,5},{5,9},{9,13},{13,1},{2,6},{6,10},{... | collective-permute-start | bytes 3538952 | tf_op jit(solution)/shard_map/ppermute | solution.py:37
  173.0 49.2 %collective-permute-start.13 = (bf16[768,3,256]{0,2,1:T(8,128)(2,1)S(1)}, bf16[768,3,256]{0,2,1:T(8,128)(2,1)S(1)}, u32[]{:S(2)}, u32[]{:S(2)}) collective-permute-start(bf16[768,3,256]{0,2,1:T(8,128)(2,1)S(1)} %copy-done.1), channel_id=1, source_target_pairs={{0,12},{4,0},{8,4},{12,8},{1,13},{5,1},{9,5},{13,9},{2,14},{6,2},{... | collective-permute-start | bytes 3538952 | tf_op jit(solution)/shard_map/ppermute | solution.py:39
  210.0 26.7 %collective-permute-start.12 = (bf16[768,3,256]{0,2,1:T(8,128)(2,1)}, bf16[768,3,256]{0,2,1:T(8,128)(2,1)S(1)}, u32[]{:S(2)}, u32[]{:S(2)}) collective-permute-start(bf16[768,3,256]{0,2,1:T(8,128)(2,1)} %collective-permute-done.11), channel_id=1, source_target_pairs={{0,4},{4,8},{8,12},{12,0},{1,5},{5,9},{9,13},{13,1},{2,6},{6,10},{... | collective-permute-start | bytes 3538952 | tf_op jit(solution)/shard_map/ppermute | solution.py:37
  215.4 79.8 %collective-permute-start.7 = (bf16[2304,3,256]{0,2,1:T(8,128)(2,1)}, bf16[2304,3,256]{0,2,1:T(8,128)(2,1)}, u32[]{:S(2)}, u32[]{:S(2)}) collective-permute-start(bf16[2304,3,256]{0,2,1:T(8,128)(2,1)} %pad_maximum_fusion.1), channel_id=1, source_target_pairs={{0,16},{16,0},{1,17},{17,1},{2,18},{18,2},{3,19},{19,3},{4,20},{20... | collective-permute-start | bytes 10616840 | tf_op jit(solution)/shard_map/ppermute | solution.py:57
  244.5 50.7 %copy-start.4 = (bf16[3072,3,128]{0,2,1:T(8,128)(2,1)S(1)}, bf16[3072,3,128]{0,2,1:T(8,128)(2,1)}, u32[]{:S(2)}) copy-start(bf16[3072,3,128]{0,2,1:T(8,128)(2,1)} %constant_dynamic-slice_fusion.21) | copy-start | bytes 7077892
  244.5 50.7 %copy-start.7 = (f32[768,384]{1,0:T(8,128)S(1)}, f32[768,384]{1,0:T(8,128)}, u32[]{:S(2)}) copy-start(f32[768,384]{1,0:T(8,128)} %fusion.24) | copy-start | bytes 3538948
  244.5 101.9 %collective-permute-start.14 = (bf16[2304,3,256]{0,2,1:T(8,128)(2,1)}, bf16[2304,3,256]{0,2,1:T(8,128)(2,1)}, u32[]{:S(2)}, u32[]{:S(2)}) collective-permute-start(bf16[2304,3,256]{0,2,1:T(8,128)(2,1)} %pad_maximum_fusion.3), channel_id=1, source_target_pairs={{0,16},{16,0},{1,17},{17,1},{2,18},{18,2},{3,19},{19,3},{4,20},{20... | collective-permute-start | bytes 10616840 | tf_op jit(solution)/shard_map/ppermute | solution.py:57
  333.7 12.7 %copy-start.10 = (bf16[768,768]{1,0:T(8,128)(2,1)S(1)}, bf16[768,768]{1,0:T(8,128)(2,1)}, u32[]{:S(2)}) copy-start(bf16[768,768]{1,0:T(8,128)(2,1)} %get-tuple-element.38) | copy-start | bytes 3538948
  333.7 12.7 %copy-start.12 = (bf16[768,768]{1,0:T(8,128)(2,1)S(1)}, bf16[768,768]{1,0:T(8,128)(2,1)}, u32[]{:S(2)}) copy-start(bf16[768,768]{1,0:T(8,128)(2,1)} %get-tuple-element.39) | copy-start | bytes 3538948
  333.7 12.7 %copy-start.14 = (bf16[768,768]{1,0:T(8,128)(2,1)S(1)}, bf16[768,768]{1,0:T(8,128)(2,1)}, u32[]{:S(2)}) copy-start(bf16[768,768]{1,0:T(8,128)(2,1)} %get-tuple-element.40) | copy-start | bytes 3538948
  371.7 4.4 collective-permute-start.15
  372.1 5.3 %collective-permute-start.16 = (bf16[48,768]{1,0:T(8,128)(2,1)S(1)}, bf16[48,768]{1,0:T(8,128)(2,1)S(1)}, u32[]{:S(2)}, u32[]{:S(2)}) collective-permute-start(bf16[48,768]{1,0:T(8,128)(2,1)S(1)} %get-tuple-element.74), channel_id=1, source_target_pairs={{0,8},{4,12},{8,0},{12,4},{1,9},{5,13},{9,1},{13,5},{2,10},{6,14},... | collective-permute-start | bytes 221192 | tf_op jit(solution)/shard_map/ppermute | solution.py:147
  373.1 5.8 %collective-permute-start.17 = (bf16[48,768]{1,0:T(8,128)(2,1)S(1)}, bf16[48,768]{1,0:T(8,128)(2,1)S(1)}, u32[]{:S(2)}, u32[]{:S(2)}) collective-permute-start(bf16[48,768]{1,0:T(8,128)(2,1)S(1)} %get-tuple-element.74), channel_id=1, source_target_pairs={{0,12},{4,0},{8,4},{12,8},{1,13},{5,1},{9,5},{13,9},{2,14},{6,2},{... | collective-permute-start | bytes 221192 | tf_op jit(solution)/shard_map/ppermute | solution.py:147
  383.2 8.8 %collective-permute-start.18 = (bf16[48,3,1024]{2,0,1:T(8,128)(2,1)S(1)}, bf16[48,3,1024]{2,0,1:T(8,128)(2,1)S(1)}, u32[]{:S(2)}, u32[]{:S(2)}) collective-permute-start(bf16[48,3,1024]{2,0,1:T(8,128)(2,1)S(1)} %get-tuple-element.68), channel_id=1, source_target_pairs={{0,1},{1,2},{2,3},{3,0},{4,5},{5,6},{6,7},{7,4},{8,9},{9,10},{10,1... | collective-permute-start | bytes 884744 | tf_op jit(solution)/shard_map/ppermute | solution.py:163
  383.3 9.9 %collective-permute-start.19 = (bf16[48,3,1024]{2,0,1:T(8,128)(2,1)S(1)}, bf16[48,3,1024]{2,0,1:T(8,128)(2,1)S(1)}, u32[]{:S(2)}, u32[]{:S(2)}) collective-permute-start(bf16[48,3,1024]{2,0,1:T(8,128)(2,1)S(1)} %get-tuple-element.70), channel_id=1, source_target_pairs={{0,2},{1,3},{2,0},{3,1},{4,6},{5,7},{6,4},{7,5},{8,10},{9,11},{10,... | collective-permute-start | bytes 884744 | tf_op jit(solution)/shard_map/ppermute | solution.py:163
  383.9 13.1 %collective-permute-start.20 = (bf16[48,3,1024]{2,0,1:T(8,128)(2,1)S(1)}, bf16[48,3,1024]{2,0,1:T(8,128)(2,1)S(1)}, u32[]{:S(2)}, u32[]{:S(2)}) collective-permute-start(bf16[48,3,1024]{2,0,1:T(8,128)(2,1)S(1)} %get-tuple-element.69), channel_id=1, source_target_pairs={{0,3},{1,0},{2,1},{3,2},{4,7},{5,4},{6,5},{7,6},{8,11},{9,8},{10,9... | collective-permute-start | bytes 884744 | tf_op jit(solution)/shard_map/ppermute | solution.py:163
  397.2 21.8 %collective-permute-start.21 = (bf16[48,3,1024]{2,0,1:T(8,128)(2,1)S(1)}, bf16[48,3,1024]{2,0,1:T(8,128)(2,1)S(1)}, u32[]{:S(2)}, u32[]{:S(2)}) collective-permute-start(bf16[48,3,1024]{2,0,1:T(8,128)(2,1)S(1)} %add_convert_fusion), channel_id=1, source_target_pairs={{0,0},{1,4},{2,8},{3,12},{4,1},{5,5},{6,9},{7,13},{8,2},{9,6},{10,... | collective-permute-start | bytes 884744 | tf_op jit(solution)/shard_map/ppermute | solution.py:174
  401.4 26.9 %collective-permute-start.22 = (bf16[48,3,1024]{2,0,1:T(8,128)(2,1)S(1)}, bf16[48,3,1024]{2,0,1:T(8,128)(2,1)S(1)}, u32[]{:S(2)}, u32[]{:S(2)}) collective-permute-start(bf16[48,3,1024]{2,0,1:T(8,128)(2,1)S(1)} %add_convert_fusion), channel_id=1, source_target_pairs={{0,4},{1,8},{2,12},{3,0},{4,5},{5,9},{6,13},{7,1},{8,6},{9,10},{10... | collective-permute-start | bytes 884744 | tf_op jit(solution)/shard_map/ppermute | solution.py:174
  404.1 24.2 %collective-permute-start.23 = (bf16[48,3,1024]{2,0,1:T(8,128)(2,1)S(1)}, bf16[48,3,1024]{2,0,1:T(8,128)(2,1)S(1)}, u32[]{:S(2)}, u32[]{:S(2)}) collective-permute-start(bf16[48,3,1024]{2,0,1:T(8,128)(2,1)S(1)} %add_convert_fusion), channel_id=1, source_target_pairs={{0,8},{1,12},{2,0},{3,4},{4,9},{5,13},{6,1},{7,5},{8,10},{9,14},{1... | collective-permute-start | bytes 884744 | tf_op jit(solution)/shard_map/ppermute | solution.py:174
  404.1 26.2 %collective-permute-start.24 = (bf16[48,3,1024]{2,0,1:T(8,128)(2,1)S(1)}, bf16[48,3,1024]{2,0,1:T(8,128)(2,1)S(1)}, u32[]{:S(2)}, u32[]{:S(2)}) collective-permute-start(bf16[48,3,1024]{2,0,1:T(8,128)(2,1)S(1)} %add_convert_fusion), channel_id=1, source_target_pairs={{0,12},{1,0},{2,4},{3,8},{4,13},{5,1},{6,5},{7,9},{8,14},{9,2},{10... | collective-permute-start | bytes 884744 | tf_op jit(solution)/shard_map/ppermute | solution.py:174
  (14 other events, 88.0 us)
Sparse Core Ops, SparseCore 0:
  250.0 87.8 all-gather.1
